TPU v7x, 32 devices: a whole 2x2x4 slice. The times are simulated.
32 devices in a mesh: outer: 4 (over y, core), inner: 8 (over z, x).
Axes of the slice: x: 2, y: 2, z: 4, core: 2. Of those that a mesh axis runs over, the one named last changes fastest.
Arguments:
- queries: bfloat16 [4, 8, 8, 64, 512], P('outer', None, 'inner'), may hold values from -240 to 240
- keys: bfloat16 [4, 8, 8, 64, 128], P('outer', None, 'inner'), may hold values from -6 to 6
- values: bfloat16 [4, 8, 8, 64, 128], P('outer', None, 'inner'), may hold values from -6 to 6
- grad_out: bfloat16 [4, 8, 8, 64, 512], P('outer', None, 'inner'), may hold values from -6 to 6
- doc_starts: int32 [4, 8, 4], replicated, may hold values from 0 to 512, as said below
Outputs:
- attn_out: bfloat16 [4, 8, 8, 64, 512], P('outer', None, 'inner')
- query_grads: bfloat16 [4, 8, 8, 64, 512], P('outer', None, 'inner')
- key_grads: bfloat16 [4, 8, 8, 64, 128], P('outer', None, 'inner')
- value_grads: bfloat16 [4, 8, 8, 64, 128], P('outer', None, 'inner')
Inputs may be any that keep to these rules, and one draw needn't show every extreme that they name: `doc_starts`: entry [o, u, j] is an offset within unit u of segment o at which a document starts, or 512 for none. The offsets below 512 of a unit are distinct, rise with j and stand before all its 512 entries. Offset 0 starts a document in every even unit except unit 0 of segments o > 0; unit 0 of such a segment and an odd unit may continue the document of the position before them (then their first entry is not 0). The last unit of every segment continues the one before it; position 0 of the sequence starts a document.
All inputs are finite; a program needn't handle non-finite values.
Results may differ from a plain program's by a relative error of at most 0.0075.
Values may be sent and summed in bfloat16 or wider, within the bound.
No kernel may reach another device: no remote copies, remote signals or barrier semaphores. Data moves between devices by JAX's collectives and lax.ppermute only.
A program may use at most 128 MiB of HBM per device.

v0:
```python
import math
import jax
import jax.numpy as jnp
from jax import lax
from jax.sharding import PartitionSpec as P


def passed_along(x, axis, by):
    size = lax.axis_size(axis)
    pairs = [(i, i + by) for i in range(size) if 0 <= i + by < size]
    return lax.ppermute(x, axis, pairs)


def doc_table(doc_starts, tok_dev):
    n_outer, n_inner, n_slots = doc_starts.shape
    flat_starts = doc_starts.reshape(n_outer * n_inner, n_slots)
    start_counts = jnp.sum((flat_starts < tok_dev).astype(jnp.int32), axis=1)
    first_index = jnp.cumsum(start_counts) - start_counts
    offsets = jnp.arange(tok_dev, dtype=jnp.int32)
    inside_count = jnp.sum(
        (flat_starts[:, None, :] <= offsets[None, :, None]).astype(jnp.int32), axis=2
    )
    return (first_index[:, None] + inside_count - 1).reshape(n_outer, n_inner, tok_dev)


def owner_table(doc_starts):
    n_outer, n_inner = (doc_starts.shape[0], doc_starts.shape[1])
    pairs = n_inner // 2
    joined = (doc_starts[:, 1::2, 0] != 0).astype(jnp.int32)
    pair_ids = jnp.arange(pairs, dtype=jnp.int32)
    relative = jnp.where(pair_ids == 0, 0, jnp.where(pair_ids == pairs - 1, 1, pair_ids + 1))
    pair_owner = (jnp.arange(n_outer, dtype=jnp.int32)[:, None] + relative[None, :]) % pairs
    even_owner = 2 * pair_owner
    owner = jnp.stack([even_owner, even_owner + 1 - joined], axis=2)
    return owner.reshape(n_outer, n_inner)


def slot_table(unit_owner):
    n_inner = unit_owner.shape[1]
    same_owner = unit_owner[:, :, None] == unit_owner[:, None, :]
    earlier = jnp.arange(n_inner)[None, :] < jnp.arange(n_inner)[:, None]
    return jnp.sum((same_owner & earlier[None]).astype(jnp.int32), axis=2)


def route_table(target_row, slot_row, slot_count):
    n_units = target_row.shape[0]
    unit_ids = jnp.arange(n_units, dtype=jnp.int32)
    tables = []
    for slot_id in range(slot_count):
        matched = (target_row[None, :] == unit_ids[:, None]) & (slot_row[None, :] == slot_id)
        present = jnp.any(matched, axis=1)
        chosen = jnp.sum(jnp.where(matched, unit_ids[None, :], 0), axis=1)
        tables.append(jnp.where(present, chosen, n_units))
    return jnp.stack(tables)


def pack_rows(piece_rows, index_table):
    padded = jnp.concatenate(
        [piece_rows, jnp.zeros((1,) + piece_rows.shape[1:], piece_rows.dtype)], axis=0
    )
    return padded[index_table]


def unpack(arrived, target_row, slot_row):
    n_slots, n_inner = (arrived.shape[0], arrived.shape[1])
    flat_rows = arrived.reshape((n_slots * n_inner,) + arrived.shape[2:])
    return flat_rows[slot_row * n_inner + target_row]


def holder_meta(owner_row, slot_row, docs_row, holder, seg_start, is_valid, missing):
    n_inner, tok_dev = docs_row.shape
    unit_ids = jnp.arange(n_inner, dtype=jnp.int32)
    offsets = jnp.arange(tok_dev, dtype=jnp.int32)
    places, labels = ([], [])
    for slot_id in range(2):
        matched = (owner_row == holder) & (slot_row == slot_id)
        unit_id = jnp.sum(jnp.where(matched, unit_ids, 0))
        present = jnp.any(matched) & is_valid
        places.append(seg_start + unit_id * tok_dev + offsets)
        labels.append(jnp.where(present, docs_row[unit_id], missing))
    return (jnp.concatenate(places), jnp.concatenate(labels))


def attend(
    query_buf, grad_buf, query_pos, query_doc, key_buf, value_buf, key_pos, key_doc, n_heads
):
    n_rows = query_buf.shape[0]
    head_dim = key_buf.shape[1]
    scaling = 1.0 / math.sqrt(head_dim)
    q_three = query_buf.reshape(n_rows, n_heads, head_dim)
    g_three = grad_buf.reshape(n_rows, n_heads, head_dim)
    scores = (
        jnp.einsum("qhd,kd->hqk", q_three, key_buf, preferred_element_type=jnp.float32) * scaling
    )
    allowed = (query_doc[:, None] == key_doc[None, :]) & (key_pos[None, :] <= query_pos[:, None])
    scores = jnp.where(allowed[None], scores, -jnp.inf)
    row_max = jnp.max(scores, axis=2, keepdims=True)
    log_total = row_max + jnp.log(jnp.sum(jnp.exp(scores - row_max), axis=2, keepdims=True))
    probs = jnp.exp(scores - log_total)
    probs_low = probs.astype(jnp.bfloat16)
    attn = jnp.einsum(
        "hqk,kd->qhd", probs_low, value_buf, preferred_element_type=jnp.float32
    ).astype(jnp.bfloat16)
    inner_prod = jnp.sum(g_three.astype(jnp.float32) * attn.astype(jnp.float32), axis=2)
    grad_probs = jnp.einsum("qhd,kd->hqk", g_three, value_buf, preferred_element_type=jnp.float32)
    score_grads = (probs * (grad_probs - inner_prod.T[:, :, None])).astype(jnp.bfloat16)
    q_grads = (
        jnp.einsum("hqk,kd->qhd", score_grads, key_buf, preferred_element_type=jnp.float32)
        * scaling
    )
    k_grads = (
        jnp.einsum("hqk,qhd->kd", score_grads, q_three, preferred_element_type=jnp.float32)
        * scaling
    )
    v_grads = jnp.einsum("hqk,qhd->kd", probs_low, g_three, preferred_element_type=jnp.float32)
    return (
        attn.reshape(n_rows, -1),
        q_grads.astype(jnp.bfloat16).reshape(n_rows, -1),
        k_grads,
        v_grads,
    )


def shards(queries, keys, values, grad_out, doc_starts):
    n_inner = lax.axis_size("inner")
    piece_len = queries.shape[3]
    width_q = queries.shape[4]
    head_dim = keys.shape[4]
    n_heads = width_q // head_dim
    tok_dev = piece_len * n_inner
    seg_len = tok_dev * n_inner
    outer_id = lax.axis_index("outer")
    inner_id = lax.axis_index("inner")
    unit_owner = owner_table(doc_starts)
    slot_all = slot_table(unit_owner)
    docs_all = doc_table(doc_starts, tok_dev)
    own_owner = unit_owner[outer_id]
    own_slot = slot_all[outer_id]
    own_docs = docs_all[outer_id]
    before = jnp.maximum(outer_id - 1, 0)
    prev_owner = unit_owner[before]
    prev_slot = slot_all[before]
    prev_docs = docs_all[before]
    has_before = outer_id > 0
    seg_start = outer_id * seg_len
    prev_start = before * seg_len
    query_rows = queries[0, :, 0]
    key_rows = keys[0, :, 0]
    value_rows = values[0, :, 0]
    grad_rows = grad_out[0, :, 0]
    hold_index = route_table(own_owner, own_slot, 2)
    q_in, k_in, v_in, g_in = (
        lax.all_to_all(
            pack_rows(query_rows, hold_index), "inner", split_axis=1, concat_axis=1, tiled=True
        ),
        lax.all_to_all(
            pack_rows(key_rows, hold_index), "inner", split_axis=1, concat_axis=1, tiled=True
        ),
        lax.all_to_all(
            pack_rows(value_rows, hold_index), "inner", split_axis=1, concat_axis=1, tiled=True
        ),
        lax.all_to_all(
            pack_rows(grad_rows, hold_index), "inner", split_axis=1, concat_axis=1, tiled=True
        ),
    )
    query_buf = q_in.reshape(2 * tok_dev, width_q)
    grad_buf = g_in.reshape(2 * tok_dev, width_q)
    key_buf = k_in.reshape(2 * tok_dev, head_dim)
    value_buf = v_in.reshape(2 * tok_dev, head_dim)
    prev_keys, prev_values = passed_along((key_buf, value_buf), "outer", 1)
    query_pos, query_doc = holder_meta(
        own_owner, own_slot, own_docs, inner_id, seg_start, outer_id >= 0, -1
    )
    ctx_keys = jnp.concatenate([key_buf, prev_keys])
    ctx_values = jnp.concatenate([value_buf, prev_values])
    own_pos, own_doc = holder_meta(
        own_owner, own_slot, own_docs, inner_id, seg_start, outer_id >= 0, -1
    )
    back_pos, back_doc = holder_meta(
        prev_owner, prev_slot, prev_docs, inner_id, prev_start, has_before, -2
    )
    key_pos = jnp.concatenate([own_pos, back_pos])
    key_doc = jnp.concatenate([own_doc, back_doc])
    attn, q_grads, k_grads, v_grads = attend(
        query_buf, grad_buf, query_pos, query_doc, ctx_keys, ctx_values, key_pos, key_doc, n_heads
    )
    later_kg, later_vg = passed_along((k_grads[2 * tok_dev :], v_grads[2 * tok_dev :]), "outer", -1)
    key_total = (
        (k_grads[: 2 * tok_dev] + later_kg)
        .astype(jnp.bfloat16)
        .reshape(2, n_inner, piece_len, head_dim)
    )
    value_total = (
        (v_grads[: 2 * tok_dev] + later_vg)
        .astype(jnp.bfloat16)
        .reshape(2, n_inner, piece_len, head_dim)
    )
    attn_back, qg_back, kg_back, vg_back = (
        lax.all_to_all(
            attn.reshape(2, n_inner, piece_len, width_q),
            "inner",
            split_axis=1,
            concat_axis=1,
            tiled=True,
        ),
        lax.all_to_all(
            q_grads.reshape(2, n_inner, piece_len, width_q),
            "inner",
            split_axis=1,
            concat_axis=1,
            tiled=True,
        ),
        lax.all_to_all(key_total, "inner", split_axis=1, concat_axis=1, tiled=True),
        lax.all_to_all(value_total, "inner", split_axis=1, concat_axis=1, tiled=True),
    )
    attn_rows = unpack(attn_back, own_owner, own_slot)
    qgrad_rows = unpack(qg_back, own_owner, own_slot)
    kgrad_rows = unpack(kg_back, own_owner, own_slot)
    vgrad_rows = unpack(vg_back, own_owner, own_slot)
    shape_q = (1, n_inner, 1, piece_len, width_q)
    shape_k = (1, n_inner, 1, piece_len, head_dim)
    return (
        attn_rows.reshape(shape_q),
        qgrad_rows.reshape(shape_q),
        kgrad_rows.reshape(shape_k),
        vgrad_rows.reshape(shape_k),
    )


def solution(mesh):
    return jax.shard_map(
        shards,
        mesh=mesh,
        in_specs=(
            P("outer", None, "inner", None, None),
            P("outer", None, "inner", None, None),
            P("outer", None, "inner", None, None),
            P("outer", None, "inner", None, None),
            P(),
        ),
        out_specs=(
            P("outer", None, "inner", None, None),
            P("outer", None, "inner", None, None),
            P("outer", None, "inner", None, None),
            P("outer", None, "inner", None, None),
        ),
        check_vma=False,
    )
```

profile of v0, /device:TPU:0, one launch (start us, length us, event | category | flops | bytes accessed | tf_op | source)
XLA Modules:
  0.0 296.2 jit_solution(16554586157267958369)
XLA Ops:
  5.2 7.3 %all-to-all-start.1 = ((bf16[2,8,64,128]{3,2,0,1:T(8,128)(2,1)}), bf16[2,8,64,128]{3,2,0,1:T(8,128)(2,1)S(1)}, u32[]{:S(2)}, u32[]{:S(2)}) async-start(bf16[2,8,64,128]{3,2,0,1:T(8,128)(2,1)} %copy.125), calls=%async_computation.1 | async-start | bytes 524288 | tf_op jit(solution)/shard_map/all_to_all | solution.py:156
  14.8 6.7 %all-to-all-done.1 = bf16[2,8,64,128]{3,2,0,1:T(8,128)(2,1)S(1)} async-done(((bf16[2,8,64,128]{3,2,0,1:T(8,128)(2,1)}), bf16[2,8,64,128]{3,2,0,1:T(8,128)(2,1)S(1)}, u32[]{:S(2)}, u32[]{:S(2)}) %all-to-all-start.1) | async-done | bytes 262176 | tf_op jit(solution)/shard_map/all_to_all | solution.py:156
  21.4 3.6 %all-to-all-start = ((bf16[2,8,64,128]{3,2,0,1:T(8,128)(2,1)}), bf16[2,8,64,128]{3,2,0,1:T(8,128)(2,1)S(1)}, u32[]{:S(2)}, u32[]{:S(2)}) async-start(bf16[2,8,64,128]{3,2,0,1:T(8,128)(2,1)} %copy.118), calls=%async_computation | async-start | bytes 524288 | tf_op jit(solution)/shard_map/all_to_all | solution.py:159
  27.9 5.7 %all-to-all-done = bf16[2,8,64,128]{3,2,0,1:T(8,128)(2,1)S(1)} async-done(((bf16[2,8,64,128]{3,2,0,1:T(8,128)(2,1)}), bf16[2,8,64,128]{3,2,0,1:T(8,128)(2,1)S(1)}, u32[]{:S(2)}, u32[]{:S(2)}) %all-to-all-start) | async-done | bytes 262176 | tf_op jit(solution)/shard_map/all_to_all | solution.py:159
  33.6 3.6 %all-to-all-start.2 = ((bf16[2,8,64,512]{3,2,0,1:T(8,128)(2,1)}), bf16[2,8,64,512]{3,2,0,1:T(8,128)(2,1)S(1)}, u32[]{:S(2)}, u32[]{:S(2)}) async-start(bf16[2,8,64,512]{3,2,0,1:T(8,128)(2,1)} %copy.127), calls=%async_computation.2 | async-start | bytes 2097152 | tf_op jit(solution)/shard_map/all_to_all | solution.py:153
  42.0 20.7 %all-to-all-done.2 = bf16[2,8,64,512]{3,2,0,1:T(8,128)(2,1)S(1)} async-done(((bf16[2,8,64,512]{3,2,0,1:T(8,128)(2,1)}), bf16[2,8,64,512]{3,2,0,1:T(8,128)(2,1)S(1)}, u32[]{:S(2)}, u32[]{:S(2)}) %all-to-all-start.2) | async-done | bytes 1048608 | tf_op jit(solution)/shard_map/all_to_all | solution.py:153
  62.7 3.6 %all-to-all-start.4 = ((bf16[2,8,64,512]{3,2,0,1:T(8,128)(2,1)}), bf16[2,8,64,512]{3,2,0,1:T(8,128)(2,1)S(1)}, u32[]{:S(2)}, u32[]{:S(2)}) async-start(bf16[2,8,64,512]{3,2,0,1:T(8,128)(2,1)} %copy.134), calls=%async_computation.4 | async-start | bytes 2097152 | tf_op jit(solution)/shard_map/all_to_all | solution.py:162
  81.7 2.2 collective-permute-start.1
  83.9 2.3 compare_and_fusion
  89.9 4.0 %collective-permute-start = (bf16[1024,128]{0,1:T(8,128)(2,1)}, bf16[1024,128]{0,1:T(8,128)(2,1)}, u32[]{:S(2)}, u32[]{:S(2)}) collective-permute-start(bf16[1024,128]{0,1:T(8,128)(2,1)} %copy.121), channel_id=1, source_target_pairs={{0,8},{8,16},{16,24},{1,9},{9,17},{17,25},{2,10},{10,18},{18,26},{... | collective-permute-start | bytes 786440 | tf_op jit(solution)/shard_map/ppermute | solution.py:11
  93.9 2.3 copy.128
  96.2 2.1 reshape_reshape.12
  98.4 2.9 copy.164
  101.3 3.2 %reshape.537 = bf16[1024,4,128]{0,2,1:T(8,128)(2,1)S(1)} reshape(bf16[2,8,64,512]{2,1,0,3:T(8,128)(2,1)} %copy.164) | data formatting | bytes 2097152 | tf_op jit(solution)/shard_map/reshape;reshape | solution.py:91
  104.5 15.2 %fusion.3 = (f32[4,1024]{1,0:T(4,128)S(1)}, f32[2048,1024,4]{1,0,2:T(8,128)}) fusion(pred[1024,2048]{0,1:T(8,128)(4,1)S(1)} %compare_and_fusion, bf16[1024,4,128]{2,1,0:T(4,128)(2,1)} %reshape_reshape.12, bf16[1024,128]{1,0:T(8,128)(2,1)} %collective-permute-done.1, bf16[1024,128]{1,0:T(8,128)(2,1)S(1)} %bitcast.128), kind=kOutput, calls=%fused_computation.15 | convolution fusion | flops 2173693952 | bytes 37240832 | tf_op jit(solution)/shard_map/qhd,kd->hqk/dot_general | solution.py:93
  119.8 14.3 %exponential_reduce_fusion = f32[4,1024]{1,0:T(4,128)S(1)} fusion(f32[2048,1024,4]{1,0,2:T(8,128)} %get-tuple-element.44, f32[4,1024]{1,0:T(4,128)S(1)} %get-tuple-element.43, pred[1024,2048]{0,1:T(8,128)(4,1)S(1)} %compare_and_fusion), kind=kLoop, calls=%fused_computation.13 | loop fusion | flops 33550336 | bytes 35684352 | tf_op jit(solution)/shard_map/reduce_sum | solution.py:98
  134.1 15.2 %convolution_bitcast_fusion = f32[2048,128]{1,0:T(8,128)} fusion(bf16[1024,4,128]{0,2,1:T(8,128)(2,1)S(1)} %reshape.537, f32[2048,1024,4]{1,0,2:T(8,128)} %get-tuple-element.44, f32[4,1024]{1,0:T(4,128)S(1)} %log_add_fusion, pred[1024,2048]{0,1:T(8,128)(4,1)S(1)} %compare_and_fusion), kind=kOutput, calls=%fused_computation.17 | convolution fusion | flops 2181038080 | bytes 37765120 | tf_op jit(solution)/shard_map/hqk,qhd->kd/dot_general | solution.py:115
  152.7 16.4 %multiply_reduce_fusion = (f32[1024,4]{0,1:T(4,128)S(1)}, bf16[1024,4,128]{0,2,1:T(8,128)(2,1)}) fusion(bf16[1024,4,128]{0,2,1:T(8,128)(2,1)S(1)} %reshape.537, f32[2048,1024,4]{1,0,2:T(8,128)} %get-tuple-element.44, f32[4,1024]{1,0:T(4,128)S(1)} %log_add_fusion, pred[1024,2048]{0,1:T(8,128)(4,1)S(1)} %compare_and_fusion, ...), kind=kOutput, calls=%fused_computation.21 | convolution fusion | flops 2184704000 | bytes 38305792 | tf_op jit(solution)/shard_map/hqk,kd->qhd/dot_general | solution.py:101
  169.1 16.5 %fusion.1 = bf16[4,1024,2048]{1,2,0:T(8,128)(2,1)S(1)} fusion(f32[2048,1024,4]{1,0,2:T(8,128)} %get-tuple-element.44, bf16[1024,4,128]{0,2,1:T(8,128)(2,1)} %copy-done.3, f32[4,1024]{1,0:T(4,128)S(1)} %bitcast.152, f32[4,1024]{1,0:T(4,128)S(1)} %log_add_fusion, pred[1024,2048]{0,1:T(8,128)(4,1)} %copy-done.1, bf16[1024,128]{0,1:T(8,128)(2,1)} %collective-permute-done, ...), kind=kOutput, calls=%fused_computation.10 | convolution fusion | flops 2198863872 | bytes 54034432 | tf_op jit(solution)/shard_map/qhd,kd->hqk/dot_general | solution.py:105
  185.6 5.7 %copy-done = bf16[4,1024,2048]{1,2,0:T(8,128)(2,1)} copy-done((bf16[4,1024,2048]{1,2,0:T(8,128)(2,1)}, bf16[4,1024,2048]{1,2,0:T(8,128)(2,1)S(1)}, u32[]{:S(2)}) %copy-start) | copy-done | bytes 16777240
  191.3 6.0 %fusion.4 = f32[2048,128]{1,0:T(8,128)S(1)} fusion(bf16[4,1024,2048]{1,2,0:T(8,128)(2,1)S(1)} %fusion.1, bf16[1024,4,128]{2,1,0:T(4,128)(2,1)} %reshape_reshape.12), kind=kOutput, calls=%fused_computation.19 | convolution fusion | flops 2147745792 | bytes 18874368 | tf_op jit(solution)/shard_map/hqk,qhd->kd/dot_general | solution.py:112
  200.6 5.9 %all-to-all-start.7 = ((bf16[2,8,64,128]{3,2,0,1:T(8,128)(2,1)}), bf16[2,8,64,128]{3,2,0,1:T(8,128)(2,1)S(1)}, u32[]{:S(2)}, u32[]{:S(2)}) async-start(bf16[2,8,64,128]{3,2,0,1:T(8,128)(2,1)} %copy.148), calls=%async_computation.7 | async-start | bytes 524288 | tf_op jit(solution)/shard_map/all_to_all | solution.py:214
  208.4 7.6 %all-to-all-done.7 = bf16[2,8,64,128]{3,2,0,1:T(8,128)(2,1)S(1)} async-done(((bf16[2,8,64,128]{3,2,0,1:T(8,128)(2,1)}), bf16[2,8,64,128]{3,2,0,1:T(8,128)(2,1)S(1)}, u32[]{:S(2)}, u32[]{:S(2)}) %all-to-all-start.7) | async-done | bytes 262176 | tf_op jit(solution)/shard_map/all_to_all | solution.py:214
  216.8 4.4 %all-to-all-start.6 = ((bf16[2,8,64,128]{3,2,0,1:T(8,128)(2,1)}), bf16[2,8,64,128]{3,2,0,1:T(8,128)(2,1)}, u32[]{:S(2)}, u32[]{:S(2)}) async-start(bf16[2,8,64,128]{3,2,0,1:T(8,128)(2,1)} %copy.145), calls=%async_computation.6 | async-start | bytes 524288 | tf_op jit(solution)/shard_map/all_to_all | solution.py:213
  221.1 8.3 %fusion.6 = bf16[1024,4,128]{0,2,1:T(8,128)(2,1)S(1)} fusion(bf16[4,1024,2048]{1,2,0:T(8,128)(2,1)} %copy-done, bf16[1024,128]{1,0:T(8,128)(2,1)} %collective-permute-done.1, bf16[1024,128]{1,0:T(8,128)(2,1)S(1)} %bitcast.129), kind=kOutput, calls=%fused_computation.24 | convolution fusion | flops 2149580800 | bytes 18350080 | tf_op jit(solution)/shard_map/hqk,kd->qhd/dot_general | solution.py:108
  230.8 2.5 copy.142
  233.3 6.0 %all-to-all-start.5 = ((bf16[2,8,64,512]{3,2,0,1:T(8,128)(2,1)}), bf16[2,8,64,512]{3,2,0,1:T(8,128)(2,1)S(1)}, u32[]{:S(2)}, u32[]{:S(2)}) async-start(bf16[2,8,64,512]{3,2,0,1:T(8,128)(2,1)} %copy.142), calls=%async_computation.5 | async-start | bytes 2097152 | tf_op jit(solution)/shard_map/all_to_all | solution.py:206
  239.3 3.0 reshape.528
  242.2 2.5 copy.132
  244.7 20.4 %all-to-all-done.5 = bf16[2,8,64,512]{3,2,0,1:T(8,128)(2,1)S(1)} async-done(((bf16[2,8,64,512]{3,2,0,1:T(8,128)(2,1)}), bf16[2,8,64,512]{3,2,0,1:T(8,128)(2,1)S(1)}, u32[]{:S(2)}, u32[]{:S(2)}) %all-to-all-start.5) | async-done | bytes 1048608 | tf_op jit(solution)/shard_map/all_to_all | solution.py:206
  265.2 3.6 %all-to-all-start.3 = ((bf16[2,8,64,512]{3,2,0,1:T(8,128)(2,1)}), bf16[2,8,64,512]{3,2,0,1:T(8,128)(2,1)S(1)}, u32[]{:S(2)}, u32[]{:S(2)}) async-start(bf16[2,8,64,512]{3,2,0,1:T(8,128)(2,1)} %copy.132), calls=%async_computation.3 | async-start | bytes 2097152 | tf_op jit(solution)/shard_map/all_to_all | solution.py:199
  274.7 20.1 %all-to-all-done.3 = bf16[2,8,64,512]{3,2,0,1:T(8,128)(2,1)S(1)} async-done(((bf16[2,8,64,512]{3,2,0,1:T(8,128)(2,1)}), bf16[2,8,64,512]{3,2,0,1:T(8,128)(2,1)S(1)}, u32[]{:S(2)}, u32[]{:S(2)}) %all-to-all-start.3) | async-done | bytes 1048608 | tf_op jit(solution)/shard_map/all_to_all | solution.py:199
  (92 shorter events, 39.0 us)
Async XLA Ops:
  5.2 16.2 %all-to-all-start.1 = ((bf16[2,8,64,128]{3,2,0,1:T(8,128)(2,1)}), bf16[2,8,64,128]{3,2,0,1:T(8,128)(2,1)S(1)}, u32[]{:S(2)}, u32[]{:S(2)}) async-start(bf16[2,8,64,128]{3,2,0,1:T(8,128)(2,1)} %copy.125), calls=%async_computation.1 | async-start | bytes 524288 | tf_op jit(solution)/shard_map/all_to_all | solution.py:156
  21.4 3.6 %copy-start.5 = (bf16[2,8,64,128]{3,2,0,1:T(8,128)(2,1)}, bf16[2,8,64,128]{3,2,0,1:T(8,128)(2,1)S(1)}, u32[]{:S(2)}) copy-start(bf16[2,8,64,128]{3,2,0,1:T(8,128)(2,1)S(1)} %all-to-all-done.1) | copy-start | bytes 786436
  21.4 12.2 %all-to-all-start = ((bf16[2,8,64,128]{3,2,0,1:T(8,128)(2,1)}), bf16[2,8,64,128]{3,2,0,1:T(8,128)(2,1)S(1)}, u32[]{:S(2)}, u32[]{:S(2)}) async-start(bf16[2,8,64,128]{3,2,0,1:T(8,128)(2,1)} %copy.118), calls=%async_computation | async-start | bytes 524288 | tf_op jit(solution)/shard_map/all_to_all | solution.py:159
  33.6 3.6 %copy-start.6 = (bf16[2,8,64,128]{3,2,0,1:T(8,128)(2,1)}, bf16[2,8,64,128]{3,2,0,1:T(8,128)(2,1)S(1)}, u32[]{:S(2)}) copy-start(bf16[2,8,64,128]{3,2,0,1:T(8,128)(2,1)S(1)} %all-to-all-done) | copy-start | bytes 786436
  33.6 29.1 %all-to-all-start.2 = ((bf16[2,8,64,512]{3,2,0,1:T(8,128)(2,1)}), bf16[2,8,64,512]{3,2,0,1:T(8,128)(2,1)S(1)}, u32[]{:S(2)}, u32[]{:S(2)}) async-start(bf16[2,8,64,512]{3,2,0,1:T(8,128)(2,1)} %copy.127), calls=%async_computation.2 | async-start | bytes 2097152 | tf_op jit(solution)/shard_map/all_to_all | solution.py:153
  62.7 19.0 %copy-start.2 = (bf16[2,8,64,512]{3,2,0,1:T(8,128)(2,1)}, bf16[2,8,64,512]{3,2,0,1:T(8,128)(2,1)S(1)}, u32[]{:S(2)}) copy-start(bf16[2,8,64,512]{3,2,0,1:T(8,128)(2,1)S(1)} %all-to-all-done.2) | copy-start | bytes 3145732
  62.7 35.7 %all-to-all-start.4 = ((bf16[2,8,64,512]{3,2,0,1:T(8,128)(2,1)}), bf16[2,8,64,512]{3,2,0,1:T(8,128)(2,1)S(1)}, u32[]{:S(2)}, u32[]{:S(2)}) async-start(bf16[2,8,64,512]{3,2,0,1:T(8,128)(2,1)} %copy.134), calls=%async_computation.4 | async-start | bytes 2097152 | tf_op jit(solution)/shard_map/all_to_all | solution.py:162
  81.7 22.8 %collective-permute-start.1 = (bf16[1024,128]{1,0:T(8,128)(2,1)S(1)}, bf16[1024,128]{1,0:T(8,128)(2,1)}, u32[]{:S(2)}, u32[]{:S(2)}) collective-permute-start(bf16[1024,128]{1,0:T(8,128)(2,1)S(1)} %bitcast.127), channel_id=1, source_target_pairs={{0,8},{8,16},{16,24},{1,9},{9,17},{17,25},{2,10},{10,18},{18,26},{... | collective-permute-start | bytes 786440 | tf_op jit(solution)/shard_map/ppermute | solution.py:11
  86.2 66.5 %copy-start.1 = (pred[1024,2048]{0,1:T(8,128)(4,1)}, pred[1024,2048]{0,1:T(8,128)(4,1)S(1)}, u32[]{:S(2)}) copy-start(pred[1024,2048]{0,1:T(8,128)(4,1)S(1)} %compare_and_fusion) | copy-start | bytes 6291460
  89.9 62.8 %collective-permute-start = (bf16[1024,128]{0,1:T(8,128)(2,1)}, bf16[1024,128]{0,1:T(8,128)(2,1)}, u32[]{:S(2)}, u32[]{:S(2)}) collective-permute-start(bf16[1024,128]{0,1:T(8,128)(2,1)} %copy.121), channel_id=1, source_target_pairs={{0,8},{8,16},{16,24},{1,9},{9,17},{17,25},{2,10},{10,18},{18,26},{... | collective-permute-start | bytes 786440 | tf_op jit(solution)/shard_map/ppermute | solution.py:11
  104.5 48.2 %copy-start.3 = (bf16[1024,4,128]{0,2,1:T(8,128)(2,1)}, bf16[1024,4,128]{0,2,1:T(8,128)(2,1)S(1)}, u32[]{:S(2)}) copy-start(bf16[1024,4,128]{0,2,1:T(8,128)(2,1)S(1)} %reshape.537) | copy-start | bytes 3145732
  151.2 47.4 %collective-permute-start.3 = (f32[1024,128]{1,0:T(8,128)}, f32[1024,128]{1,0:T(8,128)}, u32[]{:S(2)}, u32[]{:S(2)}) collective-permute-start(f32[1024,128]{1,0:T(8,128)} %slice.39), channel_id=1, source_target_pairs={{8,0},{16,8},{24,16},{9,1},{17,9},{25,17},{10,2},{18,10},{26,18},{... | collective-permute-start | bytes 1572872 | tf_op jit(solution)/shard_map/ppermute | solution.py:11
  185.6 5.7 %copy-start = (bf16[4,1024,2048]{1,2,0:T(8,128)(2,1)}, bf16[4,1024,2048]{1,2,0:T(8,128)(2,1)S(1)}, u32[]{:S(2)}) copy-start(bf16[4,1024,2048]{1,2,0:T(8,128)(2,1)S(1)} %fusion.1) | copy-start | bytes 50331652
  197.3 1.4 copy-start.4
  197.3 9.2 %collective-permute-start.2 = (f32[1024,128]{1,0:T(8,128)S(1)}, f32[1024,128]{1,0:T(8,128)S(1)}, u32[]{:S(2)}, u32[]{:S(2)}) collective-permute-start(f32[1024,128]{1,0:T(8,128)S(1)} %slice.37), channel_id=1, source_target_pairs={{8,0},{16,8},{24,16},{9,1},{17,9},{25,17},{10,2},{18,10},{26,18},{... | collective-permute-start | bytes 1572872 | tf_op jit(solution)/shard_map/ppermute | solution.py:11
  200.6 15.4 %all-to-all-start.7 = ((bf16[2,8,64,128]{3,2,0,1:T(8,128)(2,1)}), bf16[2,8,64,128]{3,2,0,1:T(8,128)(2,1)S(1)}, u32[]{:S(2)}, u32[]{:S(2)}) async-start(bf16[2,8,64,128]{3,2,0,1:T(8,128)(2,1)} %copy.148), calls=%async_computation.7 | async-start | bytes 524288 | tf_op jit(solution)/shard_map/all_to_all | solution.py:214
  216.0 0.7 copy-start.7
  216.8 16.5 %all-to-all-start.6 = ((bf16[2,8,64,128]{3,2,0,1:T(8,128)(2,1)}), bf16[2,8,64,128]{3,2,0,1:T(8,128)(2,1)}, u32[]{:S(2)}, u32[]{:S(2)}) async-start(bf16[2,8,64,128]{3,2,0,1:T(8,128)(2,1)} %copy.145), calls=%async_computation.6 | async-start | bytes 524288 | tf_op jit(solution)/shard_map/all_to_all | solution.py:213
  233.3 31.9 %all-to-all-start.5 = ((bf16[2,8,64,512]{3,2,0,1:T(8,128)(2,1)}), bf16[2,8,64,512]{3,2,0,1:T(8,128)(2,1)S(1)}, u32[]{:S(2)}, u32[]{:S(2)}) async-start(bf16[2,8,64,512]{3,2,0,1:T(8,128)(2,1)} %copy.142), calls=%async_computation.5 | async-start | bytes 2097152 | tf_op jit(solution)/shard_map/all_to_all | solution.py:206
  265.2 29.6 %all-to-all-start.3 = ((bf16[2,8,64,512]{3,2,0,1:T(8,128)(2,1)}), bf16[2,8,64,512]{3,2,0,1:T(8,128)(2,1)S(1)}, u32[]{:S(2)}, u32[]{:S(2)}) async-start(bf16[2,8,64,512]{3,2,0,1:T(8,128)(2,1)} %copy.132), calls=%async_computation.3 | async-start | bytes 2097152 | tf_op jit(solution)/shard_map/all_to_all | solution.py:199
where the time goes:
time: 298 us; the launch traced here: 296 us
  waiting for transfers between devices  81.3 us (27%)
  matrix products  77.5 us (26%)
  local copies, waits for them, and re-layouts  53.7 us (18%)
  starting transfers between devices  47 us (16%)
  other arithmetic  23.4 us (8%)
  between operations  13.4 us (4%)
    all_to_all x1, waiting for transfers between devices, shards(): lax.all_to_all(pack_rows(query_rows, hold_index), 'inner', split_axis=1,...  20.7 us
    all_to_all x1, waiting for transfers between devices, shards(): lax.all_to_all(q_grads.reshape(2, n_inner, piece_len, width_q), 'inner',...  20.4 us
    all_to_all x1, waiting for transfers between devices, shards(): lax.all_to_all(attn.reshape(2, n_inner, piece_len, width_q), 'inner', spl...  20.1 us
    dot_general x1, matrix products, attend(): jnp.einsum('qhd,kd->hqk', g_three, value_buf, preferred_element_type=jnp....  16.5 us
    dot_general x1, matrix products, attend(): jnp.einsum('hqk,kd->qhd', probs_low, value_buf, preferred_element_type=jn...  16.4 us
    dot_general x1, matrix products, attend(): jnp.einsum('qhd,kd->hqk', q_three, key_buf, preferred_element_type=jnp.fl...  15.2 us
    dot_general x1, matrix products, attend(): jnp.einsum('hqk,qhd->kd', probs_low, g_three, preferred_element_type=jnp....  15.2 us
    reduce_sum x1, other arithmetic, attend(): jnp.sum(jnp.exp(scores - row_max), axis=2, keepdims=True)  14.3 us
  transfers between devices with their start and end apart: 12, of which 6 were waited for; matrix products, arithmetic and copies ran while one was open for 48% of the time, Pallas kernels for 0%

commit v1 on v0

--- a/solution.py
+++ b/solution.py
@@ -3,6 +3,22 @@
 import jax.numpy as jnp
 from jax import lax
 from jax.sharding import PartitionSpec as P
+
+
+def pairwise_exchange(x, axis, split, join):
+    ways, here = (lax.axis_size(axis), lax.axis_index(axis))
+    width = x.shape[split] // ways
+    lengths = list(x.shape)
+    lengths[split] = width
+    height = lengths[join]
+    lengths[join] = height * ways
+    full = jnp.zeros(lengths, x.dtype)
+    for mask in range(ways):
+        part = lax.dynamic_slice_in_dim(x, (here ^ mask) * width, width, axis=split)
+        if mask:
+            part = lax.ppermute(part, axis, [(d, d ^ mask) for d in range(ways)])
+        full = lax.dynamic_update_slice_in_dim(full, part, (here ^ mask) * height, axis=join)
+    return full
 
 
 def passed_along(x, axis, by):
@@ -203,13 +219,7 @@
             concat_axis=1,
             tiled=True,
         ),
-        lax.all_to_all(
-            q_grads.reshape(2, n_inner, piece_len, width_q),
-            "inner",
-            split_axis=1,
-            concat_axis=1,
-            tiled=True,
-        ),
+        pairwise_exchange(q_grads.reshape(2, n_inner, piece_len, width_q), "inner", 1, 1),
         lax.all_to_all(key_total, "inner", split_axis=1, concat_axis=1, tiled=True),
         lax.all_to_all(value_total, "inner", split_axis=1, concat_axis=1, tiled=True),
     )

time: 298 us -> 267 us (0.90)
  waiting for transfers between devices: 81.3 us -> 39.6 us
  starting transfers between devices: 47 us -> 59.9 us
  local copies, waits for them, and re-layouts: 53.7 us -> 49.3 us
    all_to_all x1, waiting for transfers between devices: 20.7 us -> 0.01 us  [shards(): lax.all_to_all(pack_rows(query_rows, hold_index), 'inner', split_axis=1,...]
    all_to_all x1 -> x0, waiting for transfers between devices: 20.4 us -> none  [shards(): lax.all_to_all(q_grads.reshape(2, n_inner, piece_len, width_q), 'inner',...]
    all_to_all x1, waiting for transfers between devices: 20.1 us -> 0.01 us  [shards(): lax.all_to_all(attn.reshape(2, n_inner, piece_len, width_q), 'inner', spl...]
    ppermute x0 -> x7, waiting for transfers between devices: none -> 18.4 us  [pairwise_exchange(): part = lax.ppermute(part, axis, [(d, d ^ mask) for d in range(ways)])]
    ppermute x0 -> x7, starting transfers between devices: none -> 15.9 us  [pairwise_exchange(): part = lax.ppermute(part, axis, [(d, d ^ mask) for d in range(ways)])]
    all_to_all x1 -> x0, starting transfers between devices: 6 us -> none  [shards(): lax.all_to_all(q_grads.reshape(2, n_inner, piece_len, width_q), 'inner',...]
    all_to_all x1, waiting for transfers between devices: 0.01 us -> 3.74 us  [shards(): lax.all_to_all(key_total, 'inner', split_axis=1, concat_axis=1, tiled=True)]
    another operation x2 -> x1, local copies, waits for them, and re-layouts: 3.86 us -> 0.44 us  [shards(): q_grads.reshape(2, n_inner, piece_len, width_q)]
  transfers between devices with their start and end apart: 12 -> 18, of which waited for: 6 -> 6; matrix products, arithmetic and copies ran while one was open for 48% -> 53% of each run, Pallas kernels for 0% -> 0%
where the time goes in v1:
time: 267 us; the launch traced here: 264 us
  matrix products  77.5 us (29%)
  starting transfers between devices  59.9 us (22%)
  local copies, waits for them, and re-layouts  49.3 us (18%)
  waiting for transfers between devices  39.6 us (15%)
  other arithmetic  24 us (9%)
  between operations  13.3 us (5%)
    ppermute x7, waiting for transfers between devices, pairwise_exchange(): part = lax.ppermute(part, axis, [(d, d ^ mask) for d in range(ways)])  18.4 us
    dot_general x1, matrix products, attend(): jnp.einsum('qhd,kd->hqk', g_three, value_buf, preferred_element_type=jnp....  16.5 us
    dot_general x1, matrix products, attend(): jnp.einsum('hqk,kd->qhd', probs_low, value_buf, preferred_element_type=jn...  16.3 us
    ppermute x7, starting transfers between devices, pairwise_exchange(): part = lax.ppermute(part, axis, [(d, d ^ mask) for d in range(ways)])  15.9 us
    dot_general x1, matrix products, attend(): jnp.einsum('hqk,qhd->kd', probs_low, g_three, preferred_element_type=jnp....  15.6 us
    dot_general x1, matrix products, attend(): jnp.einsum('qhd,kd->hqk', q_three, key_buf, preferred_element_type=jnp.fl...  14.9 us
    reduce_sum x1, other arithmetic, attend(): jnp.sum(jnp.exp(scores - row_max), axis=2, keepdims=True)  14.3 us
    ppermute x4, starting transfers between devices, passed_along(): return lax.ppermute(x, axis, pairs)  8.98 us
  transfers between devices with their start and end apart: 18, of which 6 were waited for; matrix products, arithmetic and copies ran while one was open for 53% of the time, Pallas kernels for 0%

profile of v1, /device:TPU:0, one launch (start us, length us, event | category | flops | bytes accessed | tf_op | source)
XLA Modules:
  0.0 263.6 jit_solution(9643104295429657010)
XLA Ops:
  5.2 7.3 %all-to-all-start.1 = ((bf16[2,8,64,128]{3,2,0,1:T(8,128)(2,1)}), bf16[2,8,64,128]{3,2,0,1:T(8,128)(2,1)S(1)}, u32[]{:S(2)}, u32[]{:S(2)}) async-start(bf16[2,8,64,128]{3,2,0,1:T(8,128)(2,1)} %copy.121), calls=%async_computation.1 | async-start | bytes 524288 | tf_op jit(solution)/shard_map/all_to_all | solution.py:172
  14.8 6.7 %all-to-all-done.1 = bf16[2,8,64,128]{3,2,0,1:T(8,128)(2,1)S(1)} async-done(((bf16[2,8,64,128]{3,2,0,1:T(8,128)(2,1)}), bf16[2,8,64,128]{3,2,0,1:T(8,128)(2,1)S(1)}, u32[]{:S(2)}, u32[]{:S(2)}) %all-to-all-start.1) | async-done | bytes 262176 | tf_op jit(solution)/shard_map/all_to_all | solution.py:172
  21.4 3.6 %all-to-all-start = ((bf16[2,8,64,128]{3,2,0,1:T(8,128)(2,1)}), bf16[2,8,64,128]{3,2,0,1:T(8,128)(2,1)S(1)}, u32[]{:S(2)}, u32[]{:S(2)}) async-start(bf16[2,8,64,128]{3,2,0,1:T(8,128)(2,1)} %copy.114), calls=%async_computation | async-start | bytes 524288 | tf_op jit(solution)/shard_map/all_to_all | solution.py:175
  30.5 3.1 %all-to-all-done = bf16[2,8,64,128]{3,2,0,1:T(8,128)(2,1)S(1)} async-done(((bf16[2,8,64,128]{3,2,0,1:T(8,128)(2,1)}), bf16[2,8,64,128]{3,2,0,1:T(8,128)(2,1)S(1)}, u32[]{:S(2)}, u32[]{:S(2)}) %all-to-all-start) | async-done | bytes 262176 | tf_op jit(solution)/shard_map/all_to_all | solution.py:175
  33.6 4.2 %all-to-all-start.2 = ((bf16[2,8,64,512]{3,2,0,1:T(8,128)(2,1)}), bf16[2,8,64,512]{3,2,0,1:T(8,128)(2,1)}, u32[]{:S(2)}, u32[]{:S(2)}) async-start(bf16[2,8,64,512]{3,2,0,1:T(8,128)(2,1)} %copy.123), calls=%async_computation.2 | async-start | bytes 2097152 | tf_op jit(solution)/shard_map/all_to_all | solution.py:169
  54.1 2.3 compare_and_fusion
  59.5 2.3 copy.130
  62.7 4.2 %collective-permute-start = (bf16[1024,128]{0,1:T(8,128)(2,1)}, bf16[1024,128]{0,1:T(8,128)(2,1)}, u32[]{:S(2)}, u32[]{:S(2)}) collective-permute-start(bf16[1024,128]{0,1:T(8,128)(2,1)} %copy.117), channel_id=1, source_target_pairs={{0,8},{8,16},{16,24},{1,9},{9,17},{17,25},{2,10},{10,18},{18,26},{... | collective-permute-start | bytes 786440 | tf_op jit(solution)/shard_map/ppermute | solution.py:27
  66.9 5.9 %all-to-all-start.4 = ((bf16[2,8,64,512]{3,2,0,1:T(8,128)(2,1)}), bf16[2,8,64,512]{3,2,0,1:T(8,128)(2,1)S(1)}, u32[]{:S(2)}, u32[]{:S(2)}) async-start(bf16[2,8,64,512]{3,2,0,1:T(8,128)(2,1)} %copy.130), calls=%async_computation.4 | async-start | bytes 2097152 | tf_op jit(solution)/shard_map/all_to_all | solution.py:178
  72.8 2.3 copy.124
  77.2 14.9 %fusion.3 = (f32[4,1024]{1,0:T(4,128)S(1)}, f32[2048,1024,4]{1,0,2:T(8,128)}) fusion(pred[1024,2048]{0,1:T(8,128)(4,1)S(1)} %compare_and_fusion, bf16[1024,4,128]{2,1,0:T(4,128)(2,1)} %reshape_reshape.12, bf16[1024,128]{1,0:T(8,128)(2,1)} %collective-permute-done.1, bf16[1024,128]{1,0:T(8,128)(2,1)S(1)} %bitcast.126), kind=kOutput, calls=%fused_computation.15 | convolution fusion | flops 2173693952 | bytes 37240832 | tf_op jit(solution)/shard_map/qhd,kd->hqk/dot_general | solution.py:109
  92.1 14.3 %exponential_reduce_fusion = f32[4,1024]{1,0:T(4,128)S(1)} fusion(f32[2048,1024,4]{1,0,2:T(8,128)} %get-tuple-element.52, f32[4,1024]{1,0:T(4,128)S(1)} %get-tuple-element.51, pred[1024,2048]{0,1:T(8,128)(4,1)S(1)} %compare_and_fusion), kind=kLoop, calls=%fused_computation.13 | loop fusion | flops 33550336 | bytes 35684352 | tf_op jit(solution)/shard_map/reduce_sum | solution.py:114
  106.5 2.9 %copy.156 = bf16[2,8,64,512]{2,1,0,3:T(8,128)(2,1)} copy(bf16[2,8,64,512]{3,2,0,1:T(8,128)(2,1)S(1)} %all-to-all-done.4) | data formatting | bytes 2097152 | tf_op jit(solution)/shard_map/reshape;reshape | solution.py:107
  109.4 3.2 %reshape.536 = bf16[1024,4,128]{0,2,1:T(8,128)(2,1)S(1)} reshape(bf16[2,8,64,512]{2,1,0,3:T(8,128)(2,1)} %copy.156) | data formatting | bytes 2097152 | tf_op jit(solution)/shard_map/reshape;reshape | solution.py:107
  112.6 15.6 %convolution_bitcast_fusion = f32[2048,128]{1,0:T(8,128)} fusion(bf16[1024,4,128]{0,2,1:T(8,128)(2,1)S(1)} %reshape.536, f32[2048,1024,4]{1,0,2:T(8,128)} %get-tuple-element.52, f32[4,1024]{1,0:T(4,128)S(1)} %log_add_fusion, pred[1024,2048]{0,1:T(8,128)(4,1)S(1)} %compare_and_fusion), kind=kOutput, calls=%fused_computation.17 | convolution fusion | flops 2181038080 | bytes 37765120 | tf_op jit(solution)/shard_map/hqk,qhd->kd/dot_general | solution.py:131
  131.6 16.3 %multiply_reduce_fusion = (f32[1024,4]{0,1:T(4,128)S(1)}, bf16[1024,4,128]{0,2,1:T(8,128)(2,1)}) fusion(bf16[1024,4,128]{0,2,1:T(8,128)(2,1)S(1)} %reshape.536, f32[2048,1024,4]{1,0,2:T(8,128)} %get-tuple-element.52, f32[4,1024]{1,0:T(4,128)S(1)} %log_add_fusion, pred[1024,2048]{0,1:T(8,128)(4,1)S(1)} %compare_and_fusion, ...), kind=kOutput, calls=%fused_computation.21 | convolution fusion | flops 2184704000 | bytes 38305792 | tf_op jit(solution)/shard_map/hqk,kd->qhd/dot_general | solution.py:117
  148.0 16.5 %fusion.1 = bf16[4,1024,2048]{1,2,0:T(8,128)(2,1)S(1)} fusion(f32[2048,1024,4]{1,0,2:T(8,128)} %get-tuple-element.52, bf16[1024,4,128]{0,2,1:T(8,128)(2,1)} %copy-done.2, f32[4,1024]{1,0:T(4,128)S(1)} %bitcast.150, f32[4,1024]{1,0:T(4,128)S(1)} %log_add_fusion, pred[1024,2048]{0,1:T(8,128)(4,1)} %copy-done.1, bf16[1024,128]{0,1:T(8,128)(2,1)} %collective-permute-done, ...), kind=kOutput, calls=%fused_computation.10 | convolution fusion | flops 2198863872 | bytes 54034432 | tf_op jit(solution)/shard_map/qhd,kd->hqk/dot_general | solution.py:121
  164.5 5.7 %copy-done = bf16[4,1024,2048]{1,2,0:T(8,128)(2,1)} copy-done((bf16[4,1024,2048]{1,2,0:T(8,128)(2,1)}, bf16[4,1024,2048]{1,2,0:T(8,128)(2,1)S(1)}, u32[]{:S(2)}) %copy-start) | copy-done | bytes 16777240
  170.2 6.0 %fusion.4 = f32[2048,128]{1,0:T(8,128)S(1)} fusion(bf16[4,1024,2048]{1,2,0:T(8,128)(2,1)S(1)} %fusion.1, bf16[1024,4,128]{2,1,0:T(4,128)(2,1)} %reshape_reshape.12), kind=kOutput, calls=%fused_computation.19 | convolution fusion | flops 2147745792 | bytes 18874368 | tf_op jit(solution)/shard_map/hqk,qhd->kd/dot_general | solution.py:128
  179.5 6.0 %all-to-all-start.6 = ((bf16[2,8,64,128]{3,2,0,1:T(8,128)(2,1)}), bf16[2,8,64,128]{3,2,0,1:T(8,128)(2,1)S(1)}, u32[]{:S(2)}, u32[]{:S(2)}) async-start(bf16[2,8,64,128]{3,2,0,1:T(8,128)(2,1)} %copy.142), calls=%async_computation.6 | async-start | bytes 524288 | tf_op jit(solution)/shard_map/all_to_all | solution.py:224
  187.3 7.6 %all-to-all-done.6 = bf16[2,8,64,128]{3,2,0,1:T(8,128)(2,1)S(1)} async-done(((bf16[2,8,64,128]{3,2,0,1:T(8,128)(2,1)}), bf16[2,8,64,128]{3,2,0,1:T(8,128)(2,1)S(1)}, u32[]{:S(2)}, u32[]{:S(2)}) %all-to-all-start.6) | async-done | bytes 262176 | tf_op jit(solution)/shard_map/all_to_all | solution.py:224
  195.0 4.4 %all-to-all-start.5 = ((bf16[2,8,64,128]{3,2,0,1:T(8,128)(2,1)}), bf16[2,8,64,128]{3,2,0,1:T(8,128)(2,1)S(1)}, u32[]{:S(2)}, u32[]{:S(2)}) async-start(bf16[2,8,64,128]{3,2,0,1:T(8,128)(2,1)} %copy.139), calls=%async_computation.5 | async-start | bytes 524288 | tf_op jit(solution)/shard_map/all_to_all | solution.py:223
  199.4 3.0 %reshape.528 = bf16[2,8,64,512]{2,1,0,3:T(8,128)(2,1)S(1)} reshape(bf16[1024,4,128]{0,2,1:T(8,128)(2,1)} %get-tuple-element.54) | data formatting | bytes 2097152 | tf_op jit(solution)/shard_map/reshape;reshape | solution.py:216
  202.4 2.5 copy.128
  204.8 3.7 %all-to-all-done.5 = bf16[2,8,64,128]{3,2,0,1:T(8,128)(2,1)S(1)} async-done(((bf16[2,8,64,128]{3,2,0,1:T(8,128)(2,1)}), bf16[2,8,64,128]{3,2,0,1:T(8,128)(2,1)S(1)}, u32[]{:S(2)}, u32[]{:S(2)}) %all-to-all-start.5) | async-done | bytes 262176 | tf_op jit(solution)/shard_map/all_to_all | solution.py:223
  208.6 3.6 %all-to-all-start.3 = ((bf16[2,8,64,512]{3,2,0,1:T(8,128)(2,1)}), bf16[2,8,64,512]{3,2,0,1:T(8,128)(2,1)S(1)}, u32[]{:S(2)}, u32[]{:S(2)}) async-start(bf16[2,8,64,512]{3,2,0,1:T(8,128)(2,1)} %copy.128), calls=%async_computation.3 | async-start | bytes 2097152 | tf_op jit(solution)/shard_map/all_to_all | solution.py:215
  212.2 8.3 %fusion.6 = bf16[1024,4,128]{0,2,1:T(8,128)(2,1)S(1)} fusion(bf16[4,1024,2048]{1,2,0:T(8,128)(2,1)} %copy-done, bf16[1024,128]{1,0:T(8,128)(2,1)} %collective-permute-done.1, bf16[1024,128]{1,0:T(8,128)(2,1)S(1)} %bitcast.127), kind=kOutput, calls=%fused_computation.24 | convolution fusion | flops 2149580800 | bytes 18350080 | tf_op jit(solution)/shard_map/hqk,kd->qhd/dot_general | solution.py:124
  225.5 2.8 %collective-permute-start.5 = (bf16[2,1,64,512]{3,2,1,0:T(8,128)(2,1)S(1)}, bf16[2,1,64,512]{3,2,1,0:T(8,128)(2,1)S(1)}, u32[]{:S(2)}, u32[]{:S(2)}) collective-permute-start(bf16[2,1,64,512]{3,2,1,0:T(8,128)(2,1)S(1)} %get-tuple-element.38), channel_id=1, source_target_pairs={{0,4},{1,5},{2,6},{3,7},{4,0},{5,1},{6,2},{7,3},{8,12},{9,13},{10,... | collective-permute-start | bytes 393224 | tf_op jit(solution)/shard_map/ppermute | solution.py:19
  229.8 4.5 %collective-permute-start.7 = (bf16[2,1,64,512]{3,2,1,0:T(8,128)(2,1)S(1)}, bf16[2,1,64,512]{3,2,1,0:T(8,128)(2,1)S(1)}, u32[]{:S(2)}, u32[]{:S(2)}) collective-permute-start(bf16[2,1,64,512]{3,2,1,0:T(8,128)(2,1)S(1)} %get-tuple-element.36), channel_id=1, source_target_pairs={{0,6},{1,7},{2,4},{3,5},{4,2},{5,3},{6,0},{7,1},{8,14},{9,15},{10,... | collective-permute-start | bytes 393224 | tf_op jit(solution)/shard_map/ppermute | solution.py:19
  234.4 3.5 %collective-permute-start.8 = (bf16[2,1,64,512]{3,2,1,0:T(8,128)(2,1)S(1)}, bf16[2,1,64,512]{3,2,1,0:T(8,128)(2,1)S(1)}, u32[]{:S(2)}, u32[]{:S(2)}) collective-permute-start(bf16[2,1,64,512]{3,2,1,0:T(8,128)(2,1)S(1)} %get-tuple-element.35), channel_id=1, source_target_pairs={{0,7},{1,6},{2,5},{3,4},{4,3},{5,2},{6,1},{7,0},{8,15},{9,14},{10,... | collective-permute-start | bytes 393224 | tf_op jit(solution)/shard_map/ppermute | solution.py:19
  237.9 15.5 %collective-permute-done.5 = bf16[2,1,64,512]{3,2,1,0:T(8,128)(2,1)S(1)} collective-permute-done((bf16[2,1,64,512]{3,2,1,0:T(8,128)(2,1)S(1)}, bf16[2,1,64,512]{3,2,1,0:T(8,128)(2,1)S(1)}, u32[]{:S(2)}, u32[]{:S(2)}) %collective-permute-start.5) | collective-permute-done | bytes 131104 | tf_op jit(solution)/shard_map/ppermute | solution.py:19
  253.4 2.9 %collective-permute-done.6 = bf16[2,1,64,512]{3,2,1,0:T(8,128)(2,1)S(1)} collective-permute-done((bf16[2,1,64,512]{3,2,1,0:T(8,128)(2,1)S(1)}, bf16[2,1,64,512]{3,2,1,0:T(8,128)(2,1)S(1)}, u32[]{:S(2)}, u32[]{:S(2)}) %collective-permute-start.6) | collective-permute-done | bytes 131104 | tf_op jit(solution)/shard_map/ppermute | solution.py:19
  (108 shorter events, 44.7 us)
Async XLA Ops:
  5.2 16.2 %all-to-all-start.1 = ((bf16[2,8,64,128]{3,2,0,1:T(8,128)(2,1)}), bf16[2,8,64,128]{3,2,0,1:T(8,128)(2,1)S(1)}, u32[]{:S(2)}, u32[]{:S(2)}) async-start(bf16[2,8,64,128]{3,2,0,1:T(8,128)(2,1)} %copy.121), calls=%async_computation.1 | async-start | bytes 524288 | tf_op jit(solution)/shard_map/all_to_all | solution.py:172
  21.4 12.2 %all-to-all-start = ((bf16[2,8,64,128]{3,2,0,1:T(8,128)(2,1)}), bf16[2,8,64,128]{3,2,0,1:T(8,128)(2,1)S(1)}, u32[]{:S(2)}, u32[]{:S(2)}) async-start(bf16[2,8,64,128]{3,2,0,1:T(8,128)(2,1)} %copy.114), calls=%async_computation | async-start | bytes 524288 | tf_op jit(solution)/shard_map/all_to_all | solution.py:175
  33.6 33.3 %all-to-all-start.2 = ((bf16[2,8,64,512]{3,2,0,1:T(8,128)(2,1)}), bf16[2,8,64,512]{3,2,0,1:T(8,128)(2,1)}, u32[]{:S(2)}, u32[]{:S(2)}) async-start(bf16[2,8,64,512]{3,2,0,1:T(8,128)(2,1)} %copy.123), calls=%async_computation.2 | async-start | bytes 2097152 | tf_op jit(solution)/shard_map/all_to_all | solution.py:169
  52.1 25.1 %collective-permute-start.1 = (bf16[1024,128]{1,0:T(8,128)(2,1)S(1)}, bf16[1024,128]{1,0:T(8,128)(2,1)}, u32[]{:S(2)}, u32[]{:S(2)}) collective-permute-start(bf16[1024,128]{1,0:T(8,128)(2,1)S(1)} %bitcast.125), channel_id=1, source_target_pairs={{0,8},{8,16},{16,24},{1,9},{9,17},{17,25},{2,10},{10,18},{18,26},{... | collective-permute-start | bytes 786440 | tf_op jit(solution)/shard_map/ppermute | solution.py:27
  56.4 75.2 %copy-start.1 = (pred[1024,2048]{0,1:T(8,128)(4,1)}, pred[1024,2048]{0,1:T(8,128)(4,1)S(1)}, u32[]{:S(2)}) copy-start(pred[1024,2048]{0,1:T(8,128)(4,1)S(1)} %compare_and_fusion) | copy-start | bytes 6291460
  62.7 68.9 %collective-permute-start = (bf16[1024,128]{0,1:T(8,128)(2,1)}, bf16[1024,128]{0,1:T(8,128)(2,1)}, u32[]{:S(2)}, u32[]{:S(2)}) collective-permute-start(bf16[1024,128]{0,1:T(8,128)(2,1)} %copy.117), channel_id=1, source_target_pairs={{0,8},{8,16},{16,24},{1,9},{9,17},{17,25},{2,10},{10,18},{18,26},{... | collective-permute-start | bytes 786440 | tf_op jit(solution)/shard_map/ppermute | solution.py:27
  66.9 39.6 %all-to-all-start.4 = ((bf16[2,8,64,512]{3,2,0,1:T(8,128)(2,1)}), bf16[2,8,64,512]{3,2,0,1:T(8,128)(2,1)S(1)}, u32[]{:S(2)}, u32[]{:S(2)}) async-start(bf16[2,8,64,512]{3,2,0,1:T(8,128)(2,1)} %copy.130), calls=%async_computation.4 | async-start | bytes 2097152 | tf_op jit(solution)/shard_map/all_to_all | solution.py:178
  112.6 19.0 %copy-start.2 = (bf16[1024,4,128]{0,2,1:T(8,128)(2,1)}, bf16[1024,4,128]{0,2,1:T(8,128)(2,1)S(1)}, u32[]{:S(2)}) copy-start(bf16[1024,4,128]{0,2,1:T(8,128)(2,1)S(1)} %reshape.536) | copy-start | bytes 3145732
  130.1 47.4 %collective-permute-start.10 = (f32[1024,128]{1,0:T(8,128)}, f32[1024,128]{1,0:T(8,128)}, u32[]{:S(2)}, u32[]{:S(2)}) collective-permute-start(f32[1024,128]{1,0:T(8,128)} %slice.39), channel_id=1, source_target_pairs={{8,0},{16,8},{24,16},{9,1},{17,9},{25,17},{10,2},{18,10},{26,18},{... | collective-permute-start | bytes 1572872 | tf_op jit(solution)/shard_map/ppermute | solution.py:27
  164.4 5.7 %copy-start = (bf16[4,1024,2048]{1,2,0:T(8,128)(2,1)}, bf16[4,1024,2048]{1,2,0:T(8,128)(2,1)S(1)}, u32[]{:S(2)}) copy-start(bf16[4,1024,2048]{1,2,0:T(8,128)(2,1)S(1)} %fusion.1) | copy-start | bytes 50331652
  176.1 1.4 copy-start.3
  176.2 9.3 %collective-permute-start.9 = (f32[1024,128]{1,0:T(8,128)S(1)}, f32[1024,128]{1,0:T(8,128)S(1)}, u32[]{:S(2)}, u32[]{:S(2)}) collective-permute-start(f32[1024,128]{1,0:T(8,128)S(1)} %slice.37), channel_id=1, source_target_pairs={{8,0},{16,8},{24,16},{9,1},{17,9},{25,17},{10,2},{18,10},{26,18},{... | collective-permute-start | bytes 1572872 | tf_op jit(solution)/shard_map/ppermute | solution.py:27
  179.5 15.5 %all-to-all-start.6 = ((bf16[2,8,64,128]{3,2,0,1:T(8,128)(2,1)}), bf16[2,8,64,128]{3,2,0,1:T(8,128)(2,1)S(1)}, u32[]{:S(2)}, u32[]{:S(2)}) async-start(bf16[2,8,64,128]{3,2,0,1:T(8,128)(2,1)} %copy.142), calls=%async_computation.6 | async-start | bytes 524288 | tf_op jit(solution)/shard_map/all_to_all | solution.py:224
  195.0 4.4 %copy-start.4 = (bf16[2,8,64,128]{3,2,0,1:T(8,128)(2,1)}, bf16[2,8,64,128]{3,2,0,1:T(8,128)(2,1)S(1)}, u32[]{:S(2)}) copy-start(bf16[2,8,64,128]{3,2,0,1:T(8,128)(2,1)S(1)} %all-to-all-done.6) | copy-start | bytes 786436
  195.0 13.6 %all-to-all-start.5 = ((bf16[2,8,64,128]{3,2,0,1:T(8,128)(2,1)}), bf16[2,8,64,128]{3,2,0,1:T(8,128)(2,1)S(1)}, u32[]{:S(2)}, u32[]{:S(2)}) async-start(bf16[2,8,64,128]{3,2,0,1:T(8,128)(2,1)} %copy.139), calls=%async_computation.5 | async-start | bytes 524288 | tf_op jit(solution)/shard_map/all_to_all | solution.py:223
  208.6 3.6 %copy-start.5 = (bf16[2,8,64,128]{3,2,0,1:T(8,128)(2,1)}, bf16[2,8,64,128]{3,2,0,1:T(8,128)(2,1)S(1)}, u32[]{:S(2)}) copy-start(bf16[2,8,64,128]{3,2,0,1:T(8,128)(2,1)S(1)} %all-to-all-done.5) | copy-start | bytes 786436
  208.6 53.5 %all-to-all-start.3 = ((bf16[2,8,64,512]{3,2,0,1:T(8,128)(2,1)}), bf16[2,8,64,512]{3,2,0,1:T(8,128)(2,1)S(1)}, u32[]{:S(2)}, u32[]{:S(2)}) async-start(bf16[2,8,64,512]{3,2,0,1:T(8,128)(2,1)} %copy.128), calls=%async_computation.3 | async-start | bytes 2097152 | tf_op jit(solution)/shard_map/all_to_all | solution.py:215
  221.9 7.9 %collective-permute-start.2 = (bf16[2,1,64,512]{3,2,1,0:T(8,128)(2,1)S(1)}, bf16[2,1,64,512]{3,2,1,0:T(8,128)(2,1)S(1)}, u32[]{:S(2)}, u32[]{:S(2)}) collective-permute-start(bf16[2,1,64,512]{3,2,1,0:T(8,128)(2,1)S(1)} %get-tuple-element.41), channel_id=1, source_target_pairs={{0,1},{1,0},{2,3},{3,2},{4,5},{5,4},{6,7},{7,6},{8,9},{9,8},{10,11... | collective-permute-start | bytes 393224 | tf_op jit(solution)/shard_map/ppermute | solution.py:19
  224.0 10.4 %collective-permute-start.3 = (bf16[2,1,64,512]{3,2,1,0:T(8,128)(2,1)S(1)}, bf16[2,1,64,512]{3,2,1,0:T(8,128)(2,1)S(1)}, u32[]{:S(2)}, u32[]{:S(2)}) collective-permute-start(bf16[2,1,64,512]{3,2,1,0:T(8,128)(2,1)S(1)} %get-tuple-element.40), channel_id=1, source_target_pairs={{0,2},{1,3},{2,0},{3,1},{4,6},{5,7},{6,4},{7,5},{8,10},{9,11},{10,... | collective-permute-start | bytes 393224 | tf_op jit(solution)/shard_map/ppermute | solution.py:19
  225.4 12.4 %collective-permute-start.4 = (bf16[2,1,64,512]{3,2,1,0:T(8,128)(2,1)S(1)}, bf16[2,1,64,512]{3,2,1,0:T(8,128)(2,1)S(1)}, u32[]{:S(2)}, u32[]{:S(2)}) collective-permute-start(bf16[2,1,64,512]{3,2,1,0:T(8,128)(2,1)S(1)} %get-tuple-element.39), channel_id=1, source_target_pairs={{0,3},{1,2},{2,1},{3,0},{4,7},{5,6},{6,5},{7,4},{8,11},{9,10},{10,... | collective-permute-start | bytes 393224 | tf_op jit(solution)/shard_map/ppermute | solution.py:19
  225.5 27.8 %collective-permute-start.5 = (bf16[2,1,64,512]{3,2,1,0:T(8,128)(2,1)S(1)}, bf16[2,1,64,512]{3,2,1,0:T(8,128)(2,1)S(1)}, u32[]{:S(2)}, u32[]{:S(2)}) collective-permute-start(bf16[2,1,64,512]{3,2,1,0:T(8,128)(2,1)S(1)} %get-tuple-element.38), channel_id=1, source_target_pairs={{0,4},{1,5},{2,6},{3,7},{4,0},{5,1},{6,2},{7,3},{8,12},{9,13},{10,... | collective-permute-start | bytes 393224 | tf_op jit(solution)/shard_map/ppermute | solution.py:19
  228.4 27.9 %collective-permute-start.6 = (bf16[2,1,64,512]{3,2,1,0:T(8,128)(2,1)S(1)}, bf16[2,1,64,512]{3,2,1,0:T(8,128)(2,1)S(1)}, u32[]{:S(2)}, u32[]{:S(2)}) collective-permute-start(bf16[2,1,64,512]{3,2,1,0:T(8,128)(2,1)S(1)} %get-tuple-element.37), channel_id=1, source_target_pairs={{0,5},{1,4},{2,7},{3,6},{4,1},{5,0},{6,3},{7,2},{8,13},{9,12},{10,... | collective-permute-start | bytes 393224 | tf_op jit(solution)/shard_map/ppermute | solution.py:19
  229.8 26.5 %collective-permute-start.7 = (bf16[2,1,64,512]{3,2,1,0:T(8,128)(2,1)S(1)}, bf16[2,1,64,512]{3,2,1,0:T(8,128)(2,1)S(1)}, u32[]{:S(2)}, u32[]{:S(2)}) collective-permute-start(bf16[2,1,64,512]{3,2,1,0:T(8,128)(2,1)S(1)} %get-tuple-element.36), channel_id=1, source_target_pairs={{0,6},{1,7},{2,4},{3,5},{4,2},{5,3},{6,0},{7,1},{8,14},{9,15},{10,... | collective-permute-start | bytes 393224 | tf_op jit(solution)/shard_map/ppermute | solution.py:19
  234.4 22.0 %collective-permute-start.8 = (bf16[2,1,64,512]{3,2,1,0:T(8,128)(2,1)S(1)}, bf16[2,1,64,512]{3,2,1,0:T(8,128)(2,1)S(1)}, u32[]{:S(2)}, u32[]{:S(2)}) collective-permute-start(bf16[2,1,64,512]{3,2,1,0:T(8,128)(2,1)S(1)} %get-tuple-element.35), channel_id=1, source_target_pairs={{0,7},{1,6},{2,5},{3,4},{4,3},{5,2},{6,1},{7,0},{8,15},{9,14},{10,... | collective-permute-start | bytes 393224 | tf_op jit(solution)/shard_map/ppermute | solution.py:19
